TPU v7x, 256 devices: a whole 4x4x8 slice. The times are simulated.
256 devices in a mesh: dp: 8 (over x, core), expert: 32 (over y, z).
Axes of the slice: x: 4, y: 4, z: 8, core: 2. Of those that a mesh axis runs over, the one named last changes fastest.
Arguments:
- tokens: bfloat16 [8192, 2048], P(('dp', 'expert')), may hold values from -6 to 6
- expert_ids: int32 [8192, 8], P(('dp', 'expert')), may hold values from 0 to 31, all different within a row; in each aligned block of 32 rows (0 to 31, 32 to 63, ...) at most 16 rows name the same one
- gate_weights: float32 [8192, 8], P(('dp', 'expert')), may hold values from 0.05 to 0.35
- grad_output: bfloat16 [8192, 2048], P(('dp', 'expert')), may hold values from -6 to 6
- w_gate_up: bfloat16 [32, 2048, 1536], P('expert'), may hold values from -0.125 to 0.125
- w_down: bfloat16 [32, 768, 2048], P('expert'), may hold values from -0.21875 to 0.21875
Outputs:
- mixed: bfloat16 [8192, 2048], P(('dp', 'expert'))
- grad_tokens: bfloat16 [8192, 2048], P(('dp', 'expert'))
- grad_gates: float32 [8192, 8], P(('dp', 'expert'))
- grad_gate_up: float32 [32, 2048, 1536], P('expert', 'dp')
- grad_down: float32 [32, 768, 2048], P('expert', None, 'dp')
Inputs may be any that keep to these rules, and one draw needn't show every extreme that they name: `expert_ids`: in each block of 32 rows (the rows of one device) every expert is named at most 16 times, a bound that some block reaches; a row names 8 different experts, and every expert is named somewhere.
All inputs are finite; a program needn't handle non-finite values.
Results may differ from a plain program's by a relative error of at most 0.015.
Values may be sent and summed in bfloat16 or wider, within the bound.
No kernel may reach another device: no remote copies, remote signals or barrier semaphores. Data moves between devices by JAX's collectives and lax.ppermute only.
A program may use at most 128 MiB of HBM per device.

v0:
```python
import jax
import jax.numpy as jnp
from jax import lax
from jax.sharding import PartitionSpec as P


def swish_parts(gate_up, hidden_units):
    gate_half = gate_up[..., :hidden_units]
    up_half = gate_up[..., hidden_units:]
    sigmoid_part = jax.nn.sigmoid(gate_half)
    return (gate_half, up_half, sigmoid_part)


def body(tokens, expert_ids, gate_weights, grad_output, w_gate_up, w_down):
    token_count, top_count = expert_ids.shape
    width = tokens.shape[1]
    per_device = w_gate_up.shape[0]
    hidden_units = w_down.shape[1]
    owners = lax.axis_size("expert")
    expert_total = owners * per_device
    capacity = min(token_count, 2 * token_count * top_count // expert_total)
    pair_count = token_count * top_count
    me = lax.axis_index("expert")
    all_tokens = lax.all_gather(tokens, "expert", tiled=True).reshape(owners, token_count, width)
    all_ids = lax.all_gather(expert_ids, "expert", tiled=True).reshape(owners, pair_count)
    all_gates = lax.all_gather(gate_weights, "expert", tiled=True).reshape(owners, pair_count)
    all_grad = lax.all_gather(grad_output, "expert", tiled=True).reshape(owners, token_count, width)
    local_experts = me * per_device + jnp.arange(per_device, dtype=jnp.int32)
    onehot = all_ids[:, :, None] == local_experts[None, None, :]
    onehot_i = onehot.astype(jnp.int32)
    slots = jnp.cumsum(onehot_i, axis=1) - onehot_i
    slot_axis = jnp.arange(capacity, dtype=jnp.int32)
    sel = jnp.logical_and(onehot[..., None], slots[..., None] == slot_axis).transpose(2, 0, 3, 1)
    sel_f = sel.astype(jnp.float32)
    row_gate = jnp.sum(sel_f * all_gates[None, :, None, :], axis=3)
    sel_tok = jnp.sum(
        sel.reshape(per_device, owners, capacity, token_count, top_count).astype(jnp.bfloat16),
        axis=4,
    )
    x_rows = jnp.einsum(
        "jsct,std->jscd", sel_tok, all_tokens, preferred_element_type=jnp.float32
    ).astype(jnp.bfloat16)
    dy_rows = jnp.einsum("jsct,std->jscd", sel_tok, all_grad, preferred_element_type=jnp.float32)
    x_rows = x_rows.reshape(per_device, owners * capacity, width)
    dy_rows = dy_rows.reshape(per_device, owners * capacity, width)
    row_gate = row_gate.reshape(per_device, owners * capacity)
    gate_up = jnp.einsum("jrd,jdf->jrf", x_rows, w_gate_up, preferred_element_type=jnp.float32)
    gate_half, up_half, sigmoid_part = swish_parts(gate_up, hidden_units)
    swish = gate_half * sigmoid_part
    hidden = (swish * up_half).astype(jnp.bfloat16)
    out_rows = jnp.einsum(
        "jrf,jfd->jrd", hidden, w_down, preferred_element_type=jnp.float32
    ).astype(jnp.bfloat16)
    grad_rows = (row_gate[..., None] * dy_rows).astype(jnp.bfloat16)
    grad_hidden = jnp.einsum("jrd,jfd->jrf", grad_rows, w_down, preferred_element_type=jnp.float32)
    grad_gate = grad_hidden * up_half * sigmoid_part * (1.0 + gate_half * (1.0 - sigmoid_part))
    grad_up = grad_hidden * swish
    grad_act = jnp.concatenate([grad_gate, grad_up], axis=2).astype(jnp.bfloat16)
    grad_in = jnp.einsum(
        "jrf,jdf->jrd", grad_act, w_gate_up, preferred_element_type=jnp.float32
    ).astype(jnp.bfloat16)
    out_f = out_rows.astype(jnp.float32)
    row_inner = jnp.sum(out_f * dy_rows, axis=2).reshape(per_device, owners, capacity)
    gate_part = jnp.sum(sel_f * row_inner[..., None], axis=(0, 2)).reshape(
        owners * token_count, top_count
    )
    weighted = (row_gate[..., None] * out_f).astype(jnp.bfloat16)
    mixed_part = jnp.einsum(
        "jsct,jscd->std",
        sel_tok,
        weighted.reshape(per_device, owners, capacity, width),
        preferred_element_type=jnp.float32,
    ).astype(jnp.bfloat16)
    mixed = lax.psum_scatter(
        mixed_part.reshape(owners * token_count, width), "expert", scatter_dimension=0, tiled=True
    )
    grad_gates = lax.psum_scatter(gate_part, "expert", scatter_dimension=0, tiled=True)
    tokens_part = jnp.einsum(
        "jsct,jscd->std",
        sel_tok,
        grad_in.reshape(per_device, owners, capacity, width),
        preferred_element_type=jnp.float32,
    ).astype(jnp.bfloat16)
    grad_tokens = lax.psum_scatter(
        tokens_part.reshape(owners * token_count, width), "expert", scatter_dimension=0, tiled=True
    )
    down_local = jnp.einsum("jrf,jrd->jfd", hidden, grad_rows, preferred_element_type=jnp.float32)
    gate_up_local = jnp.einsum("jrd,jrf->jdf", x_rows, grad_act, preferred_element_type=jnp.float32)
    grad_gate_up = lax.psum_scatter(
        gate_up_local.astype(jnp.bfloat16), "dp", scatter_dimension=1, tiled=True
    ).astype(jnp.float32)
    grad_down = lax.psum_scatter(
        down_local.astype(jnp.bfloat16), "dp", scatter_dimension=2, tiled=True
    ).astype(jnp.float32)
    return (mixed, grad_tokens, grad_gates, grad_gate_up, grad_down)


def solution(mesh):
    in_specs = (
        P(("dp", "expert"), None),
        P(("dp", "expert"), None),
        P(("dp", "expert"), None),
        P(("dp", "expert"), None),
        P("expert", None, None),
        P("expert", None, None),
    )
    out_specs = (
        P(("dp", "expert"), None),
        P(("dp", "expert"), None),
        P(("dp", "expert"), None),
        P("expert", "dp", None),
        P("expert", None, "dp"),
    )
    return jax.shard_map(body, mesh=mesh, in_specs=in_specs, out_specs=out_specs, check_vma=False)
```

profile of v0, /device:TPU:2, one launch (start us, length us, event | category | flops | bytes accessed | tf_op | source)
XLA Modules:
  0.0 953.2 jit_solution(4402269293742463482)
XLA Ops:
  7.2 0.0 copy-start
  7.2 0.0 all-gather.5.cloned.1.call-start
  7.2 0.7 all-gather.5.cloned.1.call-update
  7.9 0.0 all-gather.7.cloned.1.call-start
  8.0 0.7 all-gather.7.cloned.1.call-update
  8.7 0.0 reduce-scatter.10.cloned.1.call-start
  8.7 46.8 %all-gather = s32[32,32,8]{1,2,0:T(8,128)S(1)} all-gather(s32[1,32,8]{1,2,0:T(8,128)} %bitcast.123), channel_id=1, replica_groups=mesh['dp'=8,'expert'=32] {'expert'}, dimensions={0}, use_global_device_ids=true | all-gather | bytes 33792 | tf_op jit(solution)/shard_map/all_gather | solution.py:25
  55.5 0.6 fusion.39
  56.2 0.1 copy.21
  56.3 0.1 copy.22
  56.4 0.6 reduce-window.6
  56.9 0.1 copy.34
  57.1 0.2 slice_reduce_fusion
  57.3 0.9 copy.20
  58.2 0.0 copy-start.6
  58.2 0.6 copy-done.6
  58.8 0.8 fusion.30
  59.6 0.2 copy.28
  59.8 42.4 %all-gather.1 = f32[32,32,8]{1,2,0:T(8,128)S(1)} all-gather(f32[1,32,8]{1,2,0:T(8,128)S(1)} %bitcast.124), channel_id=1, replica_groups=mesh['dp'=8,'expert'=32] {'expert'}, dimensions={0}, use_global_device_ids=true | all-gather | bytes 33792 | tf_op jit(solution)/shard_map/all_gather | solution.py:26
  102.2 0.8 copy.25
  103.0 4.3 convolution_convert_fusion.4
  107.3 69.6 %all-gather.7.cloned.1.call-done = bf16[1024,2048]{1,0:T(8,128)(2,1)} async-done(((bf16[32,2048]{1,0:T(8,128)(2,1)}), bf16[1024,2048]{1,0:T(8,128)(2,1)}) %all-gather.7.cloned.1.call-update) | async-done | bytes 4194320 | tf_op jit(solution)/shard_map/all_gather | solution.py:27
  176.8 3.0 fusion.44
  179.9 0.0 copy-start.1
  179.9 0.0 copy-done.4
  179.9 7.1 fusion.7
  187.0 0.5 fusion.31
  187.5 0.0 copy-start.3
  187.5 3.2 fusion.6
  190.7 0.1 mul.101
  190.7 0.1 copy.31
  190.8 1.6 select_reduce_fusion
  192.4 0.1 copy.32
  192.5 0.1 copy.26
  192.6 0.1 mul.88
  192.7 1.1 reshape.312
  193.8 0.0 reduce-scatter.10.cloned.1.call-update
  193.8 0.0 reduce-scatter.14.cloned.1.call-start
  193.9 6.0 fusion.20
  199.8 0.0 reduce-scatter.14.cloned.1.call-update
  199.8 0.2 reduce-scatter.12.cloned.1.call-start
  200.1 5.5 fusion.33
  205.6 0.0 copy-start.8
  205.6 0.0 copy-start.9
  205.6 0.9 copy-done.8
  206.5 0.3 copy-done.9
  206.7 5.5 fusion
  212.3 0.0 reduce-scatter.12.cloned.1.call-update
  212.3 0.0 reduce-scatter.6.cloned.1.call-start
  212.3 2.0 fusion.5
  214.3 3.3 convolution_convert_fusion.2
  217.7 0.0 reduce-scatter.6.cloned.1.call-update
  217.7 0.0 reduce-scatter.8.cloned.1.call-start
  217.7 6.7 fusion.17
  224.5 3.4 convolution_convert_fusion.1
  227.9 0.0 reduce-scatter.8.cloned.1.call-update
  227.9 179.2 %reduce-scatter.10.cloned.1.call-done = f32[32,8]{1,0:T(8,128)} async-done(((f32[1024,8]{1,0:T(8,128)}), f32[32,8]{1,0:T(8,128)}) %reduce-scatter.10.cloned.1.call-update) | async-done | bytes 1040 | tf_op jit(solution)/shard_map/reduce_scatter | solution.py:77
  407.1 1.4 copy.33
  408.4 34.5 %reduce-scatter.14.cloned.1.call-done = bf16[1,768,256]{2,1,0:T(8,128)(2,1)} async-done(((bf16[1,768,2048]{2,1,0:T(8,128)(2,1)}), bf16[1,768,256]{2,1,0:T(8,128)(2,1)}) %reduce-scatter.14.cloned.1.call-update) | async-done | bytes 393232 | tf_op jit(solution)/shard_map/reduce_scatter | solution.py:92
  443.0 1.9 convert_element_type.155
  444.9 45.7 %reduce-scatter.12.cloned.1.call-done = bf16[1,256,1536]{2,1,0:T(8,128)(2,1)} async-done(((bf16[1,2048,1536]{2,1,0:T(8,128)(2,1)}), bf16[1,256,1536]{2,1,0:T(8,128)(2,1)}) %reduce-scatter.12.cloned.1.call-update) | async-done | bytes 786448 | tf_op jit(solution)/shard_map/reduce_scatter | solution.py:89
  490.6 2.5 convert_element_type.152
  493.1 227.1 %reduce-scatter.6.cloned.1.call-done = bf16[32,2048]{1,0:T(8,128)(2,1)} async-done(((bf16[1024,2048]{1,0:T(8,128)(2,1)}), bf16[32,2048]{1,0:T(8,128)(2,1)}) %reduce-scatter.6.cloned.1.call-update) | async-done | bytes 131088 | tf_op jit(solution)/shard_map/reduce_scatter | solution.py:74
  720.2 226.1 %reduce-scatter.8.cloned.1.call-done = bf16[32,2048]{1,0:T(8,128)(2,1)} async-done(((bf16[1024,2048]{1,0:T(8,128)(2,1)}), bf16[32,2048]{1,0:T(8,128)(2,1)}) %reduce-scatter.8.cloned.1.call-update) | async-done | bytes 131088 | tf_op jit(solution)/shard_map/reduce_scatter | solution.py:84
  (14 shorter events, 0.1 us)
Async XLA Ops:
  7.2 180.3 %copy-start = (bf16[1,768,2048]{2,1,0:T(8,128)(2,1)S(1)}, bf16[1,768,2048]{2,1,0:T(8,128)(2,1)}, u32[]{:S(2)}) copy-start(bf16[1,768,2048]{2,1,0:T(8,128)(2,1)} %param.11) | copy-start | bytes 9437188
  7.2 52.6 %copy-start.7 = (f32[32,8]{0,1:T(8,128)S(1)}, f32[32,8]{0,1:T(8,128)}, u32[]{:S(2)}) copy-start(f32[32,8]{0,1:T(8,128)} %param.8) | copy-start | bytes 3076
  7.2 95.8 %all-gather.5.cloned.1.call-start = ((), (), s32[]{:S(2)}) async-start(), calls=%async_computation.5 | async-start | bytes 4325376 | tf_op jit(solution)/shard_map/all_gather | solution.py:24
  7.9 168.9 %all-gather.7.cloned.1.call-start = ((), (), s32[]{:S(2)}) async-start(), calls=%async_computation.7 | async-start | bytes 4325376 | tf_op jit(solution)/shard_map/all_gather | solution.py:27
  8.7 398.4 %reduce-scatter.10.cloned.1.call-start = ((), (), s32[]{:S(2)}) async-start(), calls=%async_computation.9 | async-start | bytes 540672 | tf_op jit(solution)/shard_map/reduce_scatter | solution.py:77
  58.2 0.6 copy-start.6
  176.8 3.0 copy-start.4
  179.9 7.6 copy-start.1
  186.9 3.7 copy-start.2
  187.5 3.2 copy-start.3
  193.8 249.1 %reduce-scatter.14.cloned.1.call-start = ((), (), s32[]{:S(2)}) async-start(), calls=%async_computation.11 | async-start | bytes 3538944 | tf_op jit(solution)/shard_map/reduce_scatter | solution.py:92
  199.8 290.8 %reduce-scatter.12.cloned.1.call-start = ((), (), s32[]{:S(2)}) async-start(), calls=%async_computation.10 | async-start | bytes 7077888 | tf_op jit(solution)/shard_map/reduce_scatter | solution.py:89
  200.1 6.6 copy-start.5
  205.6 0.9 copy-start.8
  205.6 1.1 copy-start.9
  212.3 507.9 %reduce-scatter.6.cloned.1.call-start = ((), (), s32[]{:S(2)}) async-start(), calls=%async_computation.6 | async-start | bytes 4325376 | tf_op jit(solution)/shard_map/reduce_scatter | solution.py:74
  217.7 728.6 %reduce-scatter.8.cloned.1.call-start = ((), (), s32[]{:S(2)}) async-start(), calls=%async_computation.8 | async-start | bytes 4325376 | tf_op jit(solution)/shard_map/reduce_scatter | solution.py:84
Sparse Core Ops, SparseCore 0:
  10.6 84.9 all-gather.4
  98.2 78.5 all-gather.6
  193.9 213.0 reduce-scatter.9
  409.5 33.4 reduce-scatter.13
  445.4 45.2 reduce-scatter.11
  494.9 225.2 reduce-scatter.5
  724.7 221.5 reduce-scatter.7
where the time goes:
time: 954 us; the launch traced here: 953 us
  waiting for transfers between devices  784 us (82%)
  blocking collectives  89.2 us (9%)
  matrix products  47.9 us (5%)
  between operations  14.3 us (1%)
  other arithmetic  10.6 us (1%)
    reduce_scatter x1, waiting for transfers between devices, body(): lax.psum_scatter(mixed_part.reshape(owners * token_count, width), 'expert...  227 us
    reduce_scatter x1, waiting for transfers between devices, body(): lax.psum_scatter(tokens_part.reshape(owners * token_count, width), 'exper...  226 us
    reduce_scatter x1, waiting for transfers between devices, body(): lax.psum_scatter(gate_part, 'expert', scatter_dimension=0, tiled=True)  179 us
    all_gather x1, waiting for transfers between devices, body(): lax.all_gather(grad_output, 'expert', tiled=True)  69.6 us
    all_gather x1, blocking collectives, body(): lax.all_gather(expert_ids, 'expert', tiled=True).reshape(owners, pair_count)  46.8 us
    reduce_scatter x1, waiting for transfers between devices, body(): lax.psum_scatter(gate_up_local.astype(jnp.bfloat16), 'dp', scatter_dimens...  45.7 us
    all_gather x1, blocking collectives, body(): lax.all_gather(gate_weights, 'expert', tiled=True)  42.4 us
    reduce_scatter x1, waiting for transfers between devices, body(): lax.psum_scatter(down_local.astype(jnp.bfloat16), 'dp', scatter_dimension...  34.5 us
  transfers between devices with their start and end apart: 7, of which 6 were waited for; matrix products, arithmetic and copies ran while one was open for 5% of the time, Pallas kernels for 0%

commit v1 on v0

--- a/solution.py
+++ b/solution.py
@@ -24,7 +24,9 @@
     all_tokens = lax.all_gather(tokens, "expert", tiled=True).reshape(owners, token_count, width)
     all_ids = lax.all_gather(expert_ids, "expert", tiled=True).reshape(owners, pair_count)
     all_gates = lax.all_gather(gate_weights, "expert", tiled=True).reshape(owners, pair_count)
-    all_grad = lax.all_gather(grad_output, "expert", tiled=True).reshape(owners, token_count, width)
+    all_grad = jnp.concatenate(
+        lax.all_to_all(jnp.stack([grad_output] * lax.axis_size("expert")), "expert", 0, 0), axis=0
+    ).reshape(owners, token_count, width)
     local_experts = me * per_device + jnp.arange(per_device, dtype=jnp.int32)
     onehot = all_ids[:, :, None] == local_experts[None, None, :]
     onehot_i = onehot.astype(jnp.int32)

time: 954 us -> 1010 us (1.059)
  blocking collectives: 89.2 us -> 194 us
  waiting for transfers between devices: 784 us -> 715 us
  starting transfers between devices: 0.46 us -> 12.2 us
    all_gather x1, blocking collectives: 46.8 us -> 152 us  [body(): lax.all_gather(expert_ids, 'expert', tiled=True).reshape(owners, pair_count)]
    all_gather x1 -> x0, waiting for transfers between devices: 69.6 us -> none  [body(): lax.all_gather(grad_output, 'expert', tiled=True)]
    all_to_all x0 -> x1, starting transfers between devices: none -> 11.7 us  [body(): lax.all_to_all(jnp.stack([grad_output] * lax.axis_size('expert')), 'exper...]
  transfers between devices with their start and end apart: 7 -> 7, of which waited for: 6 -> 5; matrix products, arithmetic and copies ran while one was open for 5% -> 6% of each run, Pallas kernels for 0% -> 0%
where the time goes in v1:
time: 1010 us; the launch traced here: 1000 us
  waiting for transfers between devices  715 us (71%)
  blocking collectives  194 us (19%)
  matrix products  45.7 us (5%)
  between operations  14.3 us (1%)
  local copies, waits for them, and re-layouts  12.3 us (1%)
  starting transfers between devices  12.2 us (1%)
  other arithmetic  11.5 us (1%)
    reduce_scatter x1, waiting for transfers between devices, body(): lax.psum_scatter(mixed_part.reshape(owners * token_count, width), 'expert...  227 us
    reduce_scatter x1, waiting for transfers between devices, body(): lax.psum_scatter(tokens_part.reshape(owners * token_count, width), 'exper...  226 us
    reduce_scatter x1, waiting for transfers between devices, body(): lax.psum_scatter(gate_part, 'expert', scatter_dimension=0, tiled=True)  180 us
    all_gather x1, blocking collectives, body(): lax.all_gather(expert_ids, 'expert', tiled=True).reshape(owners, pair_count)  152 us
    reduce_scatter x1, waiting for transfers between devices, body(): lax.psum_scatter(gate_up_local.astype(jnp.bfloat16), 'dp', scatter_dimens...  45.8 us
    all_gather x1, blocking collectives, body(): lax.all_gather(gate_weights, 'expert', tiled=True)  41.8 us
    reduce_scatter x1, waiting for transfers between devices, body(): lax.psum_scatter(down_local.astype(jnp.bfloat16), 'dp', scatter_dimension...  34.6 us
  transfers between devices with their start and end apart: 7, of which 5 were waited for; matrix products, arithmetic and copies ran while one was open for 6% of the time, Pallas kernels for 0%

profile of v1, /device:TPU:2, one launch (start us, length us, event | category | flops | bytes accessed | tf_op | source)
XLA Modules:
  0.0 1004.9 jit_solution(17495335565019682165)
XLA Ops:
  7.2 0.0 copy-start
  7.2 0.0 all-gather.4.cloned.1.call-start
  7.2 0.7 all-gather.4.cloned.1.call-update
  7.9 3.6 stack.2
  11.5 11.7 %all-to-all-start = ((bf16[32,32,2048]{2,1,0:T(8,128)(2,1)}), bf16[32,32,2048]{2,1,0:T(8,128)(2,1)}, u32[]{:S(2)}, u32[]{:S(2)}) async-start(bf16[32,32,2048]{2,1,0:T(8,128)(2,1)} %stack.2), calls=%async_computation.1 | async-start | bytes 8388608 | tf_op jit(solution)/shard_map/all_to_all | solution.py:28
  23.3 0.0 reduce-scatter.10.cloned.1.call-start
  23.3 0.0 copy-done.7
  23.3 152.4 %all-gather = s32[32,32,8]{1,2,0:T(8,128)S(1)} all-gather(s32[1,32,8]{1,2,0:T(8,128)S(1)} %bitcast.121), channel_id=1, replica_groups=mesh['dp'=8,'expert'=32] {'expert'}, dimensions={0}, use_global_device_ids=true | all-gather | bytes 33792 | tf_op jit(solution)/shard_map/all_gather | solution.py:25
  175.8 0.6 fusion.39
  176.4 0.1 copy.21
  176.5 0.1 copy.22
  176.6 0.6 reduce-window.6
  177.2 0.1 copy.34
  177.3 0.2 slice_reduce_fusion
  177.5 0.9 copy.20
  178.4 0.0 copy-start.6
  178.4 0.6 copy-done.6
  179.0 0.8 fusion.30
  179.9 0.2 copy.28
  180.0 0.0 copy-done.8
  180.0 41.8 %all-gather.1 = f32[32,32,8]{1,2,0:T(8,128)S(1)} all-gather(f32[1,32,8]{1,2,0:T(8,128)S(1)} %bitcast.122), channel_id=1, replica_groups=mesh['dp'=8,'expert'=32] {'expert'}, dimensions={0}, use_global_device_ids=true | all-gather | bytes 33792 | tf_op jit(solution)/shard_map/all_gather | solution.py:26
  221.9 0.8 copy.25
  222.6 2.9 convolution_convert_fusion.4
  225.5 6.3 fusion.7
  231.9 1.7 copy-done.2
  233.6 1.4 fusion.31
  235.0 0.0 all-to-all-done
  235.0 2.9 fusion.44
  237.9 3.2 fusion.6
  241.2 0.1 mul.101
  241.2 0.1 copy.31
  241.3 1.6 select_reduce_fusion
  243.0 0.1 copy.32
  243.0 0.1 copy.26
  243.1 0.1 mul.88
  243.2 1.1 reshape.310
  244.3 0.0 reduce-scatter.10.cloned.1.call-update
  244.3 0.0 reduce-scatter.14.cloned.1.call-start
  244.4 6.0 fusion.20
  250.3 0.0 reduce-scatter.14.cloned.1.call-update
  250.4 0.2 reduce-scatter.12.cloned.1.call-start
  250.6 5.5 fusion.33
  256.1 0.0 copy-start.9
  256.1 0.0 copy-start.10
  256.1 0.9 copy-done.9
  257.0 0.3 copy-done.10
  257.2 5.5 fusion
  262.8 0.0 reduce-scatter.12.cloned.1.call-update
  262.8 0.0 reduce-scatter.6.cloned.1.call-start
  262.8 2.0 fusion.5
  264.8 3.3 convolution_convert_fusion.2
  268.2 0.0 reduce-scatter.6.cloned.1.call-update
  268.2 0.0 reduce-scatter.8.cloned.1.call-start
  268.2 6.7 fusion.17
  275.0 3.4 convolution_convert_fusion.1
  278.3 0.0 reduce-scatter.8.cloned.1.call-update
  278.4 180.3 %reduce-scatter.10.cloned.1.call-done = f32[32,8]{1,0:T(8,128)} async-done(((f32[1024,8]{1,0:T(8,128)}), f32[32,8]{1,0:T(8,128)}) %reduce-scatter.10.cloned.1.call-update) | async-done | bytes 1040 | tf_op jit(solution)/shard_map/reduce_scatter | solution.py:79
  458.7 1.4 copy.33
  460.0 34.6 %reduce-scatter.14.cloned.1.call-done = bf16[1,768,256]{2,1,0:T(8,128)(2,1)} async-done(((bf16[1,768,2048]{2,1,0:T(8,128)(2,1)}), bf16[1,768,256]{2,1,0:T(8,128)(2,1)}) %reduce-scatter.14.cloned.1.call-update) | async-done | bytes 393232 | tf_op jit(solution)/shard_map/reduce_scatter | solution.py:94
  494.6 1.9 convert_element_type.155
  496.5 45.8 %reduce-scatter.12.cloned.1.call-done = bf16[1,256,1536]{2,1,0:T(8,128)(2,1)} async-done(((bf16[1,2048,1536]{2,1,0:T(8,128)(2,1)}), bf16[1,256,1536]{2,1,0:T(8,128)(2,1)}) %reduce-scatter.12.cloned.1.call-update) | async-done | bytes 786448 | tf_op jit(solution)/shard_map/reduce_scatter | solution.py:91
  542.3 2.5 convert_element_type.152
  544.8 227.2 %reduce-scatter.6.cloned.1.call-done = bf16[32,2048]{1,0:T(8,128)(2,1)} async-done(((bf16[1024,2048]{1,0:T(8,128)(2,1)}), bf16[32,2048]{1,0:T(8,128)(2,1)}) %reduce-scatter.6.cloned.1.call-update) | async-done | bytes 131088 | tf_op jit(solution)/shard_map/reduce_scatter | solution.py:76
  772.0 226.0 %reduce-scatter.8.cloned.1.call-done = bf16[32,2048]{1,0:T(8,128)(2,1)} async-done(((bf16[1024,2048]{1,0:T(8,128)(2,1)}), bf16[32,2048]{1,0:T(8,128)(2,1)}) %reduce-scatter.8.cloned.1.call-update) | async-done | bytes 131088 | tf_op jit(solution)/shard_map/reduce_scatter | solution.py:86
  (16 shorter events, 0.1 us)
Async XLA Ops:
  7.2 230.7 %copy-start = (bf16[1,768,2048]{2,1,0:T(8,128)(2,1)S(1)}, bf16[1,768,2048]{2,1,0:T(8,128)(2,1)}, u32[]{:S(2)}) copy-start(bf16[1,768,2048]{2,1,0:T(8,128)(2,1)} %param.11) | copy-start | bytes 9437188
  7.2 215.5 %all-gather.4.cloned.1.call-start = ((), (), s32[]{:S(2)}) async-start(), calls=%async_computation.6 | async-start | bytes 4325376 | tf_op jit(solution)/shard_map/all_gather | solution.py:24
  11.5 11.8 %copy-start.7 = (s32[32,8]{0,1:T(8,128)S(1)}, s32[32,8]{0,1:T(8,128)}, u32[]{:S(2)}) copy-start(s32[32,8]{0,1:T(8,128)} %param.7) | copy-start | bytes 3076
  11.5 168.5 %copy-start.8 = (f32[32,8]{0,1:T(8,128)S(1)}, f32[32,8]{0,1:T(8,128)}, u32[]{:S(2)}) copy-start(f32[32,8]{0,1:T(8,128)} %param.8) | copy-start | bytes 3076
  11.5 223.4 %all-to-all-start = ((bf16[32,32,2048]{2,1,0:T(8,128)(2,1)}), bf16[32,32,2048]{2,1,0:T(8,128)(2,1)}, u32[]{:S(2)}, u32[]{:S(2)}) async-start(bf16[32,32,2048]{2,1,0:T(8,128)(2,1)} %stack.2), calls=%async_computation.1 | async-start | bytes 8388608 | tf_op jit(solution)/shard_map/all_to_all | solution.py:28
  23.3 435.4 %reduce-scatter.10.cloned.1.call-start = ((), (), s32[]{:S(2)}) async-start(), calls=%async_computation.9 | async-start | bytes 540672 | tf_op jit(solution)/shard_map/reduce_scatter | solution.py:79
  178.4 0.6 copy-start.6
  225.5 6.3 copy-start.4
  231.8 1.8 copy-start.2
  235.0 3.0 copy-start.3
  237.9 3.2 copy-start.1
  244.3 250.3 %reduce-scatter.14.cloned.1.call-start = ((), (), s32[]{:S(2)}) async-start(), calls=%async_computation.11 | async-start | bytes 3538944 | tf_op jit(solution)/shard_map/reduce_scatter | solution.py:94
  250.4 291.9 %reduce-scatter.12.cloned.1.call-start = ((), (), s32[]{:S(2)}) async-start(), calls=%async_computation.10 | async-start | bytes 7077888 | tf_op jit(solution)/shard_map/reduce_scatter | solution.py:91
  250.6 6.6 copy-start.5
  256.1 0.9 copy-start.9
  256.1 1.1 copy-start.10
  262.8 509.2 %reduce-scatter.6.cloned.1.call-start = ((), (), s32[]{:S(2)}) async-start(), calls=%async_computation.7 | async-start | bytes 4325376 | tf_op jit(solution)/shard_map/reduce_scatter | solution.py:76
  268.2 729.8 %reduce-scatter.8.cloned.1.call-start = ((), (), s32[]{:S(2)}) async-start(), calls=%async_computation.8 | async-start | bytes 4325376 | tf_op jit(solution)/shard_map/reduce_scatter | solution.py:86
Sparse Core Ops, SparseCore 0:
  10.6 130.9 all-gather.3
  244.5 214.1 reduce-scatter.9
  461.2 33.3 reduce-scatter.13
  497.0 45.2 reduce-scatter.11
  546.6 225.3 reduce-scatter.5
  776.3 221.6 reduce-scatter.7
